TPU v7x, 256 devices: a whole 4x4x8 slice. The times are simulated.
256 devices in a mesh: blk: 32 (over z, y), group: 8 (over x, core).
Axes of the slice: x: 4, y: 4, z: 8, core: 2. Of those that a mesh axis runs over, the one named last changes fastest.
Arguments:
- queries: bfloat16 [32, 2048, 2560], P('blk', 'group'), may hold values from -16 to 16
- new_kv: bfloat16 [32, 2048, 512], P('blk', 'group'), may hold values from -16 to 16
- kv_pool: bfloat16 [1024, 128, 512], P('blk'), may hold values from -16 to 16
- window_table: int32 [32, 16], replicated, may hold values from 0 to 1023, as said below
- append_table: int32 [32, 16], replicated, may hold values from 0 to 1023, as said below
- cache_lengths: int32 [32], replicated, may hold values from 0 to 16384, as said below
Outputs:
- attn_out: bfloat16 [32, 2048, 2560], P('blk', 'group')
- new_pool: bfloat16 [1024, 128, 512], P('blk')
Inputs may be any that keep to these rules, and one draw needn't show every extreme that they name: `window_table`: pool page p lies on blk index p // 32. The two tables together name every pool page exactly once. For each k, each blk index holds window page k of exactly one request; at most 1 window pages of one request lie on one blk index, and some request has that many there. `append_table`: for each k, each blk index receives appended page k of exactly one request; at most one appended page of one request goes to one blk index, and some request sends one there. `cache_lengths`: A multiple of 128; some request has no cached token and some has 16384.
All inputs are finite; a program needn't handle non-finite values.
Results may differ from a plain program's by a relative error of at most 0.0043.
Values may be sent and summed in bfloat16 or wider, within the bound.
No kernel may reach another device: no remote copies, remote signals or barrier semaphores. Data moves between devices by JAX's collectives and lax.ppermute only.
A program may use at most 128 MiB of HBM per device.

v0:
```python
import jax
import jax.numpy as jnp
from jax import lax
from jax.sharding import PartitionSpec as P


def earlier_same(owners):
    slot_count = owners.shape[1]
    same_owner = owners[:, :, None] == owners[:, None, :]
    before = jnp.arange(slot_count)[None, :] < jnp.arange(slot_count)[:, None]
    return jnp.sum(same_owner & before[None, :, :], axis=2)


def pick_rows(wanted, values):
    return jnp.sum(jnp.where(wanted, values[:, None, :], 0), axis=2)


def attend(qblock, keys_use, index_use, live_use, block_start, head_count, head_size, window_len):
    block_len = qblock.shape[0]
    query_rows = qblock.reshape(block_len, head_count, head_size)
    scores = jnp.einsum(
        "thd,kd->thk", query_rows, keys_use[:, :head_size], preferred_element_type=jnp.float32
    ) * head_size ** (-0.5)
    positions = block_start + jnp.arange(block_len)
    allowed = (
        (index_use[None, :] > positions[:, None])
        & (index_use[None, :] <= positions[:, None] + window_len)
        & live_use[None, :]
    )
    scores = jnp.where(allowed[:, None, :], scores, -jnp.inf)
    row_max = jnp.max(scores, axis=2, keepdims=True)
    raw_weights = jnp.exp(scores - row_max)
    row_total = jnp.sum(raw_weights, axis=2, keepdims=True)
    weights = raw_weights.astype(jnp.bfloat16)
    weighted = jnp.einsum(
        "thk,kd->thd", weights, keys_use[:, head_size:], preferred_element_type=jnp.float32
    )
    return (weighted / row_total).astype(jnp.bfloat16).reshape(block_len, head_count * head_size)


def shards(queries, new_kv, kv_pool, window_table, append_table, cache_lengths):
    blocks = lax.axis_size("blk")
    my_block = lax.axis_index("blk")
    piece_index = lax.axis_index("group")
    tok_rows = queries.shape[1]
    per_owner = kv_pool.shape[0]
    page_rows = kv_pool.shape[1]
    key_width = kv_pool.shape[2]
    head_size = key_width // 2
    head_count = queries.shape[2] // head_size
    win_pages = window_table.shape[1]
    new_pages = append_table.shape[1]
    win_rows = win_pages * page_rows
    cap_win = (win_pages + blocks - 1) // blocks
    cap_new = (new_pages + blocks - 1) // blocks
    fresh_keys = lax.all_gather(new_kv, "group", axis=1, tiled=True)[0]
    append_rows = fresh_keys.shape[0]
    win_owner = window_table // per_owner
    win_rank = earlier_same(win_owner)
    win_wanted = (win_owner == my_block)[:, None, :] & (
        win_rank[:, None, :] == jnp.arange(cap_win)[None, :, None]
    )
    send_ids = pick_rows(win_wanted, window_table % per_owner)
    send_live = jnp.any(win_wanted, axis=2)
    own_owner = lax.dynamic_index_in_dim(win_owner, my_block, 0, keepdims=False)
    own_rank = lax.dynamic_index_in_dim(win_rank, my_block, 0, keepdims=False)
    arrival = own_owner * cap_win + own_rank
    outgoing = jnp.where(send_live[:, :, None, None], kv_pool[send_ids], 0)
    received = lax.all_to_all(
        outgoing.reshape(blocks * cap_win, page_rows, key_width),
        "blk",
        split_axis=0,
        concat_axis=0,
        tiled=True,
    )
    cached = received[arrival]
    new_owner = append_table // per_owner
    new_rank = earlier_same(new_owner)
    mine_owner = lax.dynamic_index_in_dim(new_owner, my_block, 0, keepdims=False)
    mine_rank = lax.dynamic_index_in_dim(new_rank, my_block, 0, keepdims=False)
    dest_wanted = (mine_owner[None, None, :] == jnp.arange(blocks)[:, None, None]) & (
        mine_rank[None, None, :] == jnp.arange(cap_new)[None, :, None]
    )
    page_pick = jnp.sum(jnp.where(dest_wanted, jnp.arange(new_pages)[None, None, :], 0), axis=2)
    page_live = jnp.any(dest_wanted, axis=2)
    fresh_pages = fresh_keys.reshape(new_pages, page_rows, key_width)
    parcels = jnp.where(page_live[:, :, None, None], fresh_pages[page_pick], 0)
    arrived = lax.all_to_all(
        parcels.reshape(blocks * cap_new, page_rows, key_width),
        "blk",
        split_axis=0,
        concat_axis=0,
        tiled=True,
    )
    land_wanted = (new_owner == my_block)[:, None, :] & (
        new_rank[:, None, :] == jnp.arange(cap_new)[None, :, None]
    )
    land_ids = pick_rows(land_wanted, append_table % per_owner)
    land_live = jnp.any(land_wanted, axis=2)
    targets = jnp.where(land_live, land_ids, per_owner).reshape(-1)
    new_pool = kv_pool.at[targets].set(arrived, mode="drop")
    keys_all = jnp.concatenate([cached.reshape(win_rows, key_width), fresh_keys], axis=0)
    own_length = lax.dynamic_index_in_dim(cache_lengths, my_block, 0, keepdims=False)
    filled = jnp.minimum(own_length // page_rows, win_pages)
    key_index = jnp.arange(win_rows + append_rows)
    live_keys = (key_index >= win_rows) | (key_index // page_rows >= win_pages - filled)
    block_len = min(128, tok_rows)
    block_count = tok_rows // block_len
    query_blocks = queries[0].reshape(block_count, block_len, queries.shape[2])
    first_row = piece_index * tok_rows
    offsets = jnp.arange(block_count) * block_len

    def one_block(inputs):
        qblock, offset = inputs
        block_start = first_row + offset
        return attend(
            qblock, keys_all, key_index, live_keys, block_start, head_count, head_size, win_rows
        )

    attended = lax.map(one_block, (query_blocks, offsets))
    attn_out = attended.reshape(1, tok_rows, queries.shape[2])
    return (attn_out, new_pool)


def solution(mesh):
    in_specs = (
        P("blk", "group", None),
        P("blk", "group", None),
        P("blk", None, None),
        P(),
        P(),
        P(),
    )
    out_specs = (P("blk", "group", None), P("blk", None, None))
    return jax.shard_map(shards, mesh=mesh, in_specs=in_specs, out_specs=out_specs, check_vma=False)
```

profile of v0, /device:TPU:13, one launch (start us, length us, event | category | flops | bytes accessed | tf_op | source)
XLA Modules:
  0.0 249.2 jit_solution(13082711198995688565)
XLA Ops:
  7.2 4.7 %copy.51 = bf16[32,128,512]{2,1,0:T(8,128)(2,1)} copy(bf16[32,128,512]{2,1,0:T(8,128)(2,1)} %param.10) | data formatting | bytes 8388608
  12.1 4.9 %gather_fusion = bf16[32,128,512]{2,1,0:T(8,128)(2,1)} fusion(bf16[32,128,512]{2,1,0:T(8,128)(2,1)} %copy.51, s32[1024]{0:T(1024)S(1)} %pad_clamp_fusion.2), kind=kCustom, calls=%fused_computation | custom fusion | bytes 8388736 | tf_op jit(solution)/shard_map/gather | solution.py:68
  17.0 4.5 %broadcast_select_fusion.1 = bf16[32,128,512]{2,1,0:T(8,128)(2,1)} fusion(bf16[32,128,512]{2,1,0:T(8,128)(2,1)} %gather_fusion, pred[32]{0:T(512)(128)(4,1)S(1)} %get-tuple-element.118), kind=kLoop, calls=%fused_computation.41 | loop fusion | flops 2097152 | bytes 8388640 | tf_op jit(solution)/shard_map/jit(_where)/select_n | solution.py:68
  21.5 11.3 %all-to-all-start = ((bf16[32,128,512]{2,1,0:T(8,128)(2,1)}), bf16[32,128,512]{2,1,0:T(8,128)(2,1)}, u32[]{:S(2)}, u32[]{:S(2)}) async-start(bf16[32,128,512]{2,1,0:T(8,128)(2,1)} %broadcast_select_fusion.1), calls=%async_computation | async-start | bytes 8388608 | tf_op jit(solution)/shard_map/all_to_all | solution.py:69
  38.1 26.2 %all-gather.2.cloned.1.call-done = bf16[1,2048,512]{2,1,0:T(8,128)(2,1)} async-done(((bf16[1,256,512]{2,1,0:T(8,128)(2,1)}), bf16[1,2048,512]{2,1,0:T(8,128)(2,1)}) %all-gather.2.cloned.1.call-update) | async-done | bytes 2097168 | tf_op jit(solution)/shard_map/all_gather | solution.py:56
  64.3 4.4 %gather_fusion.2 = bf16[32,128,512]{2,1,0:T(8,128)(2,1)} fusion(bf16[16,128,512]{2,1,0:T(8,128)(2,1)} %bitcast.50, s32[1024]{0:T(1024)S(1)} %pad_clamp_fusion), kind=kCustom, calls=%fused_computation.2 | custom fusion | bytes 8388736 | tf_op jit(solution)/shard_map/gather | solution.py:87
  68.7 4.5 %broadcast_select_fusion = bf16[32,128,512]{2,1,0:T(8,128)(2,1)} fusion(bf16[32,128,512]{2,1,0:T(8,128)(2,1)} %gather_fusion.2, pred[32]{0:T(512)(128)(4,1)S(1)} %fusion.35), kind=kLoop, calls=%fused_computation.40 | loop fusion | flops 2097152 | bytes 8388640 | tf_op jit(solution)/shard_map/jit(_where)/select_n | solution.py:87
  73.2 54.1 %all-to-all-done = bf16[32,128,512]{2,1,0:T(8,128)(2,1)} async-done(((bf16[32,128,512]{2,1,0:T(8,128)(2,1)}), bf16[32,128,512]{2,1,0:T(8,128)(2,1)}, u32[]{:S(2)}, u32[]{:S(2)}) %all-to-all-start) | async-done | bytes 4194336 | tf_op jit(solution)/shard_map/all_to_all | solution.py:69
  127.4 6.9 %all-to-all-start.1 = ((bf16[32,128,512]{2,1,0:T(8,128)(2,1)}), bf16[32,128,512]{2,1,0:T(8,128)(2,1)}, u32[]{:S(2)}, u32[]{:S(2)}) async-start(bf16[32,128,512]{2,1,0:T(8,128)(2,1)} %broadcast_select_fusion), calls=%async_computation.1 | async-start | bytes 8388608 | tf_op jit(solution)/shard_map/all_to_all | solution.py:88
  134.3 4.3 %gather_fusion.1 = bf16[16,128,512]{2,1,0:T(8,128)(2,1)} fusion(bf16[32,128,512]{2,1,0:T(8,128)(2,1)} %all-to-all-done, s32[1024]{0:T(1024)S(1)} %pad_clamp_fusion.1), kind=kCustom, calls=%fused_computation.1 | custom fusion | bytes 4194368 | tf_op jit(solution)/shard_map/gather | solution.py:76
  138.6 3.8 %pad_maximum_fusion = bf16[4096,512]{1,0:T(8,128)(2,1)} fusion(bf16[2048,512]{1,0:T(8,128)(2,1)S(1)} %bitcast.51, bf16[2048,512]{1,0:T(8,128)(2,1)} %bitcast.53), kind=kLoop, calls=%fused_computation.39 | loop fusion | flops 8388608 | bytes 8388608 | tf_op jit(solution)/shard_map/concatenate | solution.py:102
  142.5 45.2 %while.12 = (s32[]{:T(128)}, bf16[2,128,2560]{2,1,0:T(8,128)(2,1)}, s32[2]{0:T(128)S(1)}, s32[]{:T(128)}, bf16[2,128,2560]{2,1,0:T(8,128)(2,1)}, /*index=5*/bf16[4096,512]{1,0:T(8,128)(2,1)}, s32[]{:T(128)}, s32[]{:T(128)}) while((s32[]{:T(128)}, bf16[2,128,2560]{2,1,0:T(8,128)(2,1)}, s32[2]{0:T(128)S(1)}, s32[]{:T(128)}, ...), condition=%wide.region_6.7_spmd.clone.clone, body=%wide.region_3.6_spmd.clone.clone.sunk | while | flops 5429176320 | bytes 77106312 | solution.py:120
  144.3 1.1 constant_dynamic-slice_fusion.2
  145.8 5.1 %fusion.57 = (f32[128,10]{0,1:T(8,128)S(1)}, f32[128,10,4096]{2,0,1:T(8,128)S(1)}) fusion(pred[128,4096]{1,0:T(8,128)(4,1)S(1)} %fusion.56, bf16[128,10,256]{0,2,1:T(8,128)(2,1)S(1)} %bitcast.52, bf16[4096,512]{1,0:T(8,128)(2,1)} %get-tuple-element.198), kind=kOutput, calls=%fused_computation.8.clone.1 | convolution fusion | flops 2700081920 | bytes 24253440 | tf_op jit(solution)/shard_map/while/body/eval_jaxpr/thd,kd->thk/dot_general | solution.py:21
  150.9 6.0 %fusion.58 = f32[128,10]{0,1:T(8,128)S(1)} fusion(f32[128,10,4096]{2,0,1:T(8,128)S(1)} %get-tuple-element.175, f32[128,10]{0,1:T(8,128)S(1)} %get-tuple-element.176, pred[128,4096]{1,0:T(8,128)(4,1)S(1)} %fusion.56), kind=kLoop, calls=%fused_computation.9.clone.1 | loop fusion | flops 20970240 | bytes 21506048 | tf_op jit(solution)/shard_map/while/body/eval_jaxpr/reduce_sum | solution.py:33
  156.9 6.7 %divide_convert_fusion.2 = bf16[128,10,256]{2,0,1:T(8,128)(2,1)S(1)} fusion(bf16[4096,512]{1,0:T(8,128)(2,1)} %get-tuple-element.198, f32[128,10,4096]{2,0,1:T(8,128)S(1)} %get-tuple-element.175, f32[128,10]{0,1:T(8,128)S(1)} %get-tuple-element.176, pred[128,4096]{1,0:T(8,128)(4,1)S(1)} %fusion.56, f32[128,10]{0,1:T(8,128)S(1)} %fusion.58), kind=kOutput, calls=%fused_computation.22.clone.1 | convolution fusion | flops 2705981440 | bytes 24258560 | tf_op jit(solution)/shard_map/while/body/eval_jaxpr/thk,kd->thd/dot_general | solution.py:35
  164.2 0.9 constant_dynamic-update-slice_fusion.2
  166.9 1.1 constant_dynamic-slice_fusion.2
  168.4 5.1 %fusion.57 = (f32[128,10]{0,1:T(8,128)S(1)}, f32[128,10,4096]{2,0,1:T(8,128)S(1)}) fusion(pred[128,4096]{1,0:T(8,128)(4,1)S(1)} %fusion.56, bf16[128,10,256]{0,2,1:T(8,128)(2,1)S(1)} %bitcast.52, bf16[4096,512]{1,0:T(8,128)(2,1)} %get-tuple-element.198), kind=kOutput, calls=%fused_computation.8.clone.1 | convolution fusion | flops 2700081920 | bytes 24253440 | tf_op jit(solution)/shard_map/while/body/eval_jaxpr/thd,kd->thk/dot_general | solution.py:21
  173.4 6.0 %fusion.58 = f32[128,10]{0,1:T(8,128)S(1)} fusion(f32[128,10,4096]{2,0,1:T(8,128)S(1)} %get-tuple-element.175, f32[128,10]{0,1:T(8,128)S(1)} %get-tuple-element.176, pred[128,4096]{1,0:T(8,128)(4,1)S(1)} %fusion.56), kind=kLoop, calls=%fused_computation.9.clone.1 | loop fusion | flops 20970240 | bytes 21506048 | tf_op jit(solution)/shard_map/while/body/eval_jaxpr/reduce_sum | solution.py:33
  179.5 6.7 %divide_convert_fusion.2 = bf16[128,10,256]{2,0,1:T(8,128)(2,1)S(1)} fusion(bf16[4096,512]{1,0:T(8,128)(2,1)} %get-tuple-element.198, f32[128,10,4096]{2,0,1:T(8,128)S(1)} %get-tuple-element.175, f32[128,10]{0,1:T(8,128)S(1)} %get-tuple-element.176, pred[128,4096]{1,0:T(8,128)(4,1)S(1)} %fusion.56, f32[128,10]{0,1:T(8,128)S(1)} %fusion.58), kind=kOutput, calls=%fused_computation.22.clone.1 | convolution fusion | flops 2705981440 | bytes 24258560 | tf_op jit(solution)/shard_map/while/body/eval_jaxpr/thk,kd->thd/dot_general | solution.py:35
  186.8 0.9 constant_dynamic-update-slice_fusion.2
  187.7 44.0 %all-to-all-done.1 = bf16[32,128,512]{2,1,0:T(8,128)(2,1)} async-done(((bf16[32,128,512]{2,1,0:T(8,128)(2,1)}), bf16[32,128,512]{2,1,0:T(8,128)(2,1)}, u32[]{:S(2)}, u32[]{:S(2)}) %all-to-all-start.1) | async-done | bytes 4194336 | tf_op jit(solution)/shard_map/all_to_all | solution.py:88
  231.7 10.7 %scatter_fusion = bf16[32,128,512]{2,1,0:T(8,128)(2,1)} fusion(bf16[32,128,512]{2,1,0:T(8,128)(2,1)} %copy.51, s32[32]{0:T(128)S(1)} %copy-done.3, bf16[32,128,512]{2,1,0:T(8,128)(2,1)} %all-to-all-done.1), kind=kCustom, calls=%fused_computation.3 | custom fusion | bytes 12583040 | tf_op jit(solution)/shard_map/scatter | solution.py:101
  (48 shorter events, 7.1 us)
Async XLA Ops:
  7.2 4.7 %copy-start.1 = (s32[32,16]{0,1:T(8,128)S(1)}, s32[32,16]{0,1:T(8,128)}, u32[]{:S(2)}) copy-start(s32[32,16]{0,1:T(8,128)} %param.11) | copy-start | bytes 6148
  7.2 4.7 %copy-start.2 = (s32[32,16]{0,1:T(8,128)S(1)}, s32[32,16]{0,1:T(8,128)}, u32[]{:S(2)}) copy-start(s32[32,16]{0,1:T(8,128)} %param.12) | copy-start | bytes 6148
  21.5 12.1 %copy-start.4 = (s32[32]{0:T(128)S(1)}, s32[32]{0:T(128)}, u32[]{:S(2)}) copy-start(s32[32]{0:T(128)} %param.13) | copy-start | bytes 388
  21.5 105.9 %all-to-all-start = ((bf16[32,128,512]{2,1,0:T(8,128)(2,1)}), bf16[32,128,512]{2,1,0:T(8,128)(2,1)}, u32[]{:S(2)}, u32[]{:S(2)}) async-start(bf16[32,128,512]{2,1,0:T(8,128)(2,1)} %broadcast_select_fusion.1), calls=%async_computation | async-start | bytes 8388608 | tf_op jit(solution)/shard_map/all_to_all | solution.py:69
  32.8 31.5 %all-gather.2.cloned.1.call-start = ((), (), s32[]{:S(2)}) async-start(), calls=%async_computation.2 | async-start | bytes 2359296 | tf_op jit(solution)/shard_map/all_gather | solution.py:56
  127.4 104.3 %all-to-all-start.1 = ((bf16[32,128,512]{2,1,0:T(8,128)(2,1)}), bf16[32,128,512]{2,1,0:T(8,128)(2,1)}, u32[]{:S(2)}, u32[]{:S(2)}) async-start(bf16[32,128,512]{2,1,0:T(8,128)(2,1)} %broadcast_select_fusion), calls=%async_computation.1 | async-start | bytes 8388608 | tf_op jit(solution)/shard_map/all_to_all | solution.py:88
  134.3 4.4 %copy-start = (bf16[1,2048,512]{2,1,0:T(8,128)(2,1)S(1)}, bf16[1,2048,512]{2,1,0:T(8,128)(2,1)}, u32[]{:S(2)}) copy-start(bf16[1,2048,512]{2,1,0:T(8,128)(2,1)} %all-gather.2.cloned.1.call-done) | copy-start | bytes 6291460
  142.5 89.2 %copy-start.3 = (s32[32]{0:T(128)S(1)}, s32[32]{0:T(128)}, u32[]{:S(2)}) copy-start(s32[32]{0:T(128)} %fusion.41) | copy-start | bytes 388
Sparse Core Ops, SparseCore 0:
  35.5 28.8 all-gather.1
where the time goes:
time: 250 us; the launch traced here: 249 us
  waiting for transfers between devices  125 us (50%)
  local copies, waits for them, and re-layouts  36.9 us (15%)
  other arithmetic  27.3 us (11%)
  matrix products  23.6 us (9%)
  starting transfers between devices  18.3 us (7%)
  between operations  16.7 us (7%)
    all_to_all x1, waiting for transfers between devices, shards(): lax.all_to_all(outgoing.reshape(blocks * cap_win, page_rows, key_width),...  54.1 us
    all_to_all x1, waiting for transfers between devices, shards(): lax.all_to_all(parcels.reshape(blocks * cap_new, page_rows, key_width), '...  44 us
    all_gather x1, waiting for transfers between devices, shards(): fresh_keys = lax.all_gather(new_kv, 'group', axis=1, tiled=True)[0]  26.2 us
    dot_general x2, matrix products, attend(): jnp.einsum('thk,kd->thd', weights, keys_use[:, head_size:], preferred_ele...  13.4 us
    reduce_sum x2, other arithmetic, attend(): row_total = jnp.sum(raw_weights, axis=2, keepdims=True)  12 us
    all_to_all x1, starting transfers between devices, shards(): lax.all_to_all(outgoing.reshape(blocks * cap_win, page_rows, key_width),...  11.3 us
    scatter x1, local copies, waits for them, and re-layouts, shards(): new_pool = kv_pool.at[targets].set(arrived, mode='drop')  10.7 us
    dot_general x2, matrix products, attend(): jnp.einsum('thd,kd->thk', query_rows, keys_use[:, :head_size], preferred_...  10.2 us
  transfers between devices with their start and end apart: 3, of which 3 were waited for; matrix products, arithmetic and copies ran while one was open for 25% of the time, Pallas kernels for 0%

commit v1 on v0

--- a/solution.py
+++ b/solution.py
@@ -2,6 +2,19 @@
 import jax.numpy as jnp
 from jax import lax
 from jax.sharding import PartitionSpec as P
+
+
+def ring_gather(value, axis, dim):
+    ways = lax.axis_size(axis)
+    up = [(d, (d + 1) % ways) for d in range(ways)]
+    down = [(d, (d - 1) % ways) for d in range(ways)]
+    earlier, later = ([value], [value])
+    for _ in range(ways // 2):
+        earlier.append(lax.ppermute(earlier[-1], axis, up))
+    for _ in range((ways - 1) // 2):
+        later.append(lax.ppermute(later[-1], axis, down))
+    line = jnp.concatenate([*earlier[::-1], *later[1:]], axis=dim)
+    return jnp.roll(line, (lax.axis_index(axis) - ways // 2) * value.shape[dim], axis=dim)
 
 
 def earlier_same(owners):
@@ -53,7 +66,7 @@
     win_rows = win_pages * page_rows
     cap_win = (win_pages + blocks - 1) // blocks
     cap_new = (new_pages + blocks - 1) // blocks
-    fresh_keys = lax.all_gather(new_kv, "group", axis=1, tiled=True)[0]
+    fresh_keys = ring_gather(new_kv, "group", 1)[0]
     append_rows = fresh_keys.shape[0]
     win_owner = window_table // per_owner
     win_rank = earlier_same(win_owner)

time: 250 us -> 237 us (0.948)
  between operations: 16.7 us -> 3.18 us
  waiting for transfers between devices: 125 us -> 115 us
  starting transfers between devices: 18.3 us -> 27.7 us
  local copies, waits for them, and re-layouts: 36.9 us -> 40.3 us
    all_gather x1 -> x0, waiting for transfers between devices: 26.2 us -> none  [shards(): fresh_keys = lax.all_gather(new_kv, 'group', axis=1, tiled=True)[0]]
    ppermute x0 -> x7, waiting for transfers between devices: none -> 15.1 us  [the longest x4 9.13 us: ring_gather(): earlier.append(lax.ppermute(earlier[-1], axis, up))]
    ppermute x0 -> x7, starting transfers between devices: none -> 9.51 us  [the longest x4 9.49 us: ring_gather(): earlier.append(lax.ppermute(earlier[-1], axis, up))]
    unnamed x11 -> x30, local copies, waits for them, and re-layouts: 4.67 us -> 7.81 us
  transfers between devices with their start and end apart: 3 -> 9, of which waited for: 3 -> 6; matrix products, arithmetic and copies ran while one was open for 25% -> 26% of each run, Pallas kernels for 0% -> 0%
where the time goes in v1:
time: 237 us; the launch traced here: 236 us
  waiting for transfers between devices  115 us (49%)
  local copies, waits for them, and re-layouts  40.3 us (17%)
  starting transfers between devices  27.7 us (12%)
  other arithmetic  25.2 us (11%)
  matrix products  23.6 us (10%)
  between operations  3.18 us (1%)
    all_to_all x1, waiting for transfers between devices, shards(): lax.all_to_all(outgoing.reshape(blocks * cap_win, page_rows, key_width),...  55.3 us
    all_to_all x1, waiting for transfers between devices, shards(): lax.all_to_all(parcels.reshape(blocks * cap_new, page_rows, key_width), '...  44.1 us
    dot_general x2, matrix products, attend(): jnp.einsum('thk,kd->thd', weights, keys_use[:, head_size:], preferred_ele...  13.4 us
    reduce_sum x2, other arithmetic, attend(): row_total = jnp.sum(raw_weights, axis=2, keepdims=True)  12 us
    all_to_all x1, starting transfers between devices, shards(): lax.all_to_all(outgoing.reshape(blocks * cap_win, page_rows, key_width),...  11.3 us
    scatter x1, local copies, waits for them, and re-layouts, shards(): new_pool = kv_pool.at[targets].set(arrived, mode='drop')  10.7 us
    dot_general x2, matrix products, attend(): jnp.einsum('thd,kd->thk', query_rows, keys_use[:, :head_size], preferred_...  10.2 us
    ppermute x4, starting transfers between devices, ring_gather(): earlier.append(lax.ppermute(earlier[-1], axis, up))  9.49 us
  transfers between devices with their start and end apart: 9, of which 6 were waited for; matrix products, arithmetic and copies ran while one was open for 26% of the time, Pallas kernels for 0%

profile of v1, /device:TPU:13, one launch (start us, length us, event | category | flops | bytes accessed | tf_op | source)
XLA Modules:
  0.0 235.9 jit_solution(7794596802201944410)
XLA Ops:
  0.7 4.7 %copy.66 = bf16[32,128,512]{2,1,0:T(8,128)(2,1)} copy(bf16[32,128,512]{2,1,0:T(8,128)(2,1)} %param.10) | data formatting | bytes 8388608
  5.6 5.0 %gather_fusion = bf16[32,128,512]{2,1,0:T(8,128)(2,1)} fusion(bf16[32,128,512]{2,1,0:T(8,128)(2,1)} %copy.66, s32[1024]{0:T(1024)S(1)} %pad_clamp_fusion.2), kind=kCustom, calls=%fused_computation | custom fusion | bytes 8388736 | tf_op jit(solution)/shard_map/gather | solution.py:81
  10.5 4.5 %broadcast_select_fusion.1 = bf16[32,128,512]{2,1,0:T(8,128)(2,1)} fusion(bf16[32,128,512]{2,1,0:T(8,128)(2,1)} %gather_fusion, pred[32]{0:T(512)(128)(4,1)S(1)} %get-tuple-element.118), kind=kLoop, calls=%fused_computation.41 | loop fusion | flops 2097152 | bytes 8388640 | tf_op jit(solution)/shard_map/jit(_where)/select_n | solution.py:81
  15.0 11.3 %all-to-all-start = ((bf16[32,128,512]{2,1,0:T(8,128)(2,1)}), bf16[32,128,512]{2,1,0:T(8,128)(2,1)}, u32[]{:S(2)}, u32[]{:S(2)}) async-start(bf16[32,128,512]{2,1,0:T(8,128)(2,1)} %broadcast_select_fusion.1), calls=%async_computation | async-start | bytes 8388608 | tf_op jit(solution)/shard_map/all_to_all | solution.py:82
  29.0 2.8 %collective-permute-done = bf16[1,256,512]{2,1,0:T(8,128)(2,1)S(1)} collective-permute-done((bf16[1,256,512]{2,1,0:T(8,128)(2,1)S(1)}, bf16[1,256,512]{2,1,0:T(8,128)(2,1)S(1)}, u32[]{:S(2)}, u32[]{:S(2)}) %collective-permute-start) | collective-permute-done | bytes 262176 | tf_op jit(solution)/shard_map/ppermute | solution.py:13
  31.7 2.5 %collective-permute-start.1 = (bf16[1,256,512]{2,1,0:T(8,128)(2,1)S(1)}, bf16[1,256,512]{2,1,0:T(8,128)(2,1)S(1)}, u32[]{:S(2)}, u32[]{:S(2)}) collective-permute-start(bf16[1,256,512]{2,1,0:T(8,128)(2,1)S(1)} %collective-permute-done), channel_id=1, source_target_pairs={{0,1},{1,2},{2,3},{3,4},{4,5},{5,6},{6,7},{7,0},{8,9},{9,10},{10,1... | collective-permute-start | bytes 786440 | tf_op jit(solution)/shard_map/ppermute | solution.py:13
  34.4 3.1 %collective-permute-done.1 = bf16[1,256,512]{2,1,0:T(8,128)(2,1)S(1)} collective-permute-done((bf16[1,256,512]{2,1,0:T(8,128)(2,1)S(1)}, bf16[1,256,512]{2,1,0:T(8,128)(2,1)S(1)}, u32[]{:S(2)}, u32[]{:S(2)}) %collective-permute-start.1) | collective-permute-done | bytes 262176 | tf_op jit(solution)/shard_map/ppermute | solution.py:13
  37.5 2.5 %collective-permute-start.2 = (bf16[1,256,512]{2,1,0:T(8,128)(2,1)S(1)}, bf16[1,256,512]{2,1,0:T(8,128)(2,1)S(1)}, u32[]{:S(2)}, u32[]{:S(2)}) collective-permute-start(bf16[1,256,512]{2,1,0:T(8,128)(2,1)S(1)} %collective-permute-done.1), channel_id=1, source_target_pairs={{0,1},{1,2},{2,3},{3,4},{4,5},{5,6},{6,7},{7,0},{8,9},{9,10},{10,1... | collective-permute-start | bytes 786440 | tf_op jit(solution)/shard_map/ppermute | solution.py:13
  40.1 3.3 %collective-permute-done.2 = bf16[1,256,512]{2,1,0:T(8,128)(2,1)S(1)} collective-permute-done((bf16[1,256,512]{2,1,0:T(8,128)(2,1)S(1)}, bf16[1,256,512]{2,1,0:T(8,128)(2,1)S(1)}, u32[]{:S(2)}, u32[]{:S(2)}) %collective-permute-start.2) | collective-permute-done | bytes 262176 | tf_op jit(solution)/shard_map/ppermute | solution.py:13
  49.4 6.0 %collective-permute-done.6 = bf16[1,256,512]{2,1,0:T(8,128)(2,1)S(1)} collective-permute-done((bf16[1,256,512]{2,1,0:T(8,128)(2,1)S(1)}, bf16[1,256,512]{2,1,0:T(8,128)(2,1)S(1)}, u32[]{:S(2)}, u32[]{:S(2)}) %collective-permute-start.6) | collective-permute-done | bytes 262176 | tf_op jit(solution)/shard_map/ppermute | solution.py:15
  57.7 2.8 %gather_fusion.2 = bf16[32,128,512]{2,1,0:T(8,128)(2,1)} fusion(bf16[16,128,512]{2,1,0:T(8,128)(2,1)S(1)} %bitcast.51, s32[1024]{0:T(1024)S(1)} %pad_clamp_fusion), kind=kCustom, calls=%fused_computation.2 | custom fusion | bytes 8388736 | tf_op jit(solution)/shard_map/gather | solution.py:100
  65.6 55.3 %all-to-all-done = bf16[32,128,512]{2,1,0:T(8,128)(2,1)} async-done(((bf16[32,128,512]{2,1,0:T(8,128)(2,1)}), bf16[32,128,512]{2,1,0:T(8,128)(2,1)}, u32[]{:S(2)}, u32[]{:S(2)}) %all-to-all-start) | async-done | bytes 4194336 | tf_op jit(solution)/shard_map/all_to_all | solution.py:82
  120.9 6.9 %all-to-all-start.1 = ((bf16[32,128,512]{2,1,0:T(8,128)(2,1)}), bf16[32,128,512]{2,1,0:T(8,128)(2,1)}, u32[]{:S(2)}, u32[]{:S(2)}) async-start(bf16[32,128,512]{2,1,0:T(8,128)(2,1)} %broadcast_select_fusion), calls=%async_computation.1 | async-start | bytes 8388608 | tf_op jit(solution)/shard_map/all_to_all | solution.py:101
  127.8 4.2 %gather_fusion.1 = bf16[16,128,512]{2,1,0:T(8,128)(2,1)} fusion(bf16[32,128,512]{2,1,0:T(8,128)(2,1)} %all-to-all-done, s32[1024]{0:T(1024)S(1)} %pad_clamp_fusion.1), kind=kCustom, calls=%fused_computation.1 | custom fusion | bytes 4194368 | tf_op jit(solution)/shard_map/gather | solution.py:89
  132.0 3.8 %pad_maximum_fusion = bf16[4096,512]{1,0:T(8,128)(2,1)} fusion(bf16[2048,512]{1,0:T(8,128)(2,1)S(1)} %fusion.45, bf16[2048,512]{1,0:T(8,128)(2,1)} %bitcast.53), kind=kLoop, calls=%fused_computation.39 | loop fusion | flops 8388608 | bytes 8388608 | tf_op jit(solution)/shard_map/concatenate | solution.py:115
  135.9 45.2 %while.12 = (s32[]{:T(128)}, bf16[2,128,2560]{2,1,0:T(8,128)(2,1)}, s32[2]{0:T(128)S(1)}, s32[]{:T(128)}, bf16[2,128,2560]{2,1,0:T(8,128)(2,1)}, /*index=5*/bf16[4096,512]{1,0:T(8,128)(2,1)}, s32[]{:T(128)}, s32[]{:T(128)}) while((s32[]{:T(128)}, bf16[2,128,2560]{2,1,0:T(8,128)(2,1)}, s32[2]{0:T(128)S(1)}, s32[]{:T(128)}, ...), condition=%wide.region_6.7_spmd.clone.clone, body=%wide.region_3.6_spmd.clone.clone.sunk | while | flops 5429176320 | bytes 77106312 | solution.py:133
  139.2 5.1 %fusion.58 = (f32[128,10]{0,1:T(8,128)S(1)}, f32[128,10,4096]{2,0,1:T(8,128)S(1)}) fusion(pred[128,4096]{1,0:T(8,128)(4,1)S(1)} %fusion.57, bf16[128,10,256]{0,2,1:T(8,128)(2,1)S(1)} %bitcast.52, bf16[4096,512]{1,0:T(8,128)(2,1)} %get-tuple-element.198), kind=kOutput, calls=%fused_computation.8.clone.1 | convolution fusion | flops 2700081920 | bytes 24253440 | tf_op jit(solution)/shard_map/while/body/eval_jaxpr/thd,kd->thk/dot_general | solution.py:34
  144.3 6.0 %fusion.59 = f32[128,10]{0,1:T(8,128)S(1)} fusion(f32[128,10,4096]{2,0,1:T(8,128)S(1)} %get-tuple-element.175, f32[128,10]{0,1:T(8,128)S(1)} %get-tuple-element.176, pred[128,4096]{1,0:T(8,128)(4,1)S(1)} %fusion.57), kind=kLoop, calls=%fused_computation.9.clone.1 | loop fusion | flops 20970240 | bytes 21506048 | tf_op jit(solution)/shard_map/while/body/eval_jaxpr/reduce_sum | solution.py:46
  150.3 6.7 %divide_convert_fusion.2 = bf16[128,10,256]{2,0,1:T(8,128)(2,1)S(1)} fusion(bf16[4096,512]{1,0:T(8,128)(2,1)} %get-tuple-element.198, f32[128,10,4096]{2,0,1:T(8,128)S(1)} %get-tuple-element.175, f32[128,10]{0,1:T(8,128)S(1)} %get-tuple-element.176, pred[128,4096]{1,0:T(8,128)(4,1)S(1)} %fusion.57, f32[128,10]{0,1:T(8,128)S(1)} %fusion.59), kind=kOutput, calls=%fused_computation.22.clone.1 | convolution fusion | flops 2705981440 | bytes 24258560 | tf_op jit(solution)/shard_map/while/body/eval_jaxpr/thk,kd->thd/dot_general | solution.py:48
  161.8 5.1 %fusion.58 = (f32[128,10]{0,1:T(8,128)S(1)}, f32[128,10,4096]{2,0,1:T(8,128)S(1)}) fusion(pred[128,4096]{1,0:T(8,128)(4,1)S(1)} %fusion.57, bf16[128,10,256]{0,2,1:T(8,128)(2,1)S(1)} %bitcast.52, bf16[4096,512]{1,0:T(8,128)(2,1)} %get-tuple-element.198), kind=kOutput, calls=%fused_computation.8.clone.1 | convolution fusion | flops 2700081920 | bytes 24253440 | tf_op jit(solution)/shard_map/while/body/eval_jaxpr/thd,kd->thk/dot_general | solution.py:34
  166.9 6.0 %fusion.59 = f32[128,10]{0,1:T(8,128)S(1)} fusion(f32[128,10,4096]{2,0,1:T(8,128)S(1)} %get-tuple-element.175, f32[128,10]{0,1:T(8,128)S(1)} %get-tuple-element.176, pred[128,4096]{1,0:T(8,128)(4,1)S(1)} %fusion.57), kind=kLoop, calls=%fused_computation.9.clone.1 | loop fusion | flops 20970240 | bytes 21506048 | tf_op jit(solution)/shard_map/while/body/eval_jaxpr/reduce_sum | solution.py:46
  172.9 6.7 %divide_convert_fusion.2 = bf16[128,10,256]{2,0,1:T(8,128)(2,1)S(1)} fusion(bf16[4096,512]{1,0:T(8,128)(2,1)} %get-tuple-element.198, f32[128,10,4096]{2,0,1:T(8,128)S(1)} %get-tuple-element.175, f32[128,10]{0,1:T(8,128)S(1)} %get-tuple-element.176, pred[128,4096]{1,0:T(8,128)(4,1)S(1)} %fusion.57, f32[128,10]{0,1:T(8,128)S(1)} %fusion.59), kind=kOutput, calls=%fused_computation.22.clone.1 | convolution fusion | flops 2705981440 | bytes 24258560 | tf_op jit(solution)/shard_map/while/body/eval_jaxpr/thk,kd->thd/dot_general | solution.py:48
  181.1 44.1 %all-to-all-done.1 = bf16[32,128,512]{2,1,0:T(8,128)(2,1)} async-done(((bf16[32,128,512]{2,1,0:T(8,128)(2,1)}), bf16[32,128,512]{2,1,0:T(8,128)(2,1)}, u32[]{:S(2)}, u32[]{:S(2)}) %all-to-all-start.1) | async-done | bytes 4194336 | tf_op jit(solution)/shard_map/all_to_all | solution.py:101
  225.2 10.7 %scatter_fusion = bf16[32,128,512]{2,1,0:T(8,128)(2,1)} fusion(bf16[32,128,512]{2,1,0:T(8,128)(2,1)} %copy.66, s32[32]{0:T(128)S(1)} %copy-done.5, bf16[32,128,512]{2,1,0:T(8,128)(2,1)} %all-to-all-done.1), kind=kCustom, calls=%fused_computation.3 | custom fusion | bytes 12583040 | tf_op jit(solution)/shard_map/scatter | solution.py:114
  (81 shorter events, 22.4 us)
Async XLA Ops:
  0.6 4.7 %copy-start.3 = (s32[32,16]{0,1:T(8,128)S(1)}, s32[32,16]{0,1:T(8,128)}, u32[]{:S(2)}) copy-start(s32[32,16]{0,1:T(8,128)} %param.11) | copy-start | bytes 6148
  0.6 4.7 %copy-start.4 = (s32[32,16]{0,1:T(8,128)S(1)}, s32[32,16]{0,1:T(8,128)}, u32[]{:S(2)}) copy-start(s32[32,16]{0,1:T(8,128)} %param.12) | copy-start | bytes 6148
  15.0 11.3 %copy-start.2 = (bf16[1,256,512]{2,1,0:T(8,128)(2,1)S(1)}, bf16[1,256,512]{2,1,0:T(8,128)(2,1)}, u32[]{:S(2)}) copy-start(bf16[1,256,512]{2,1,0:T(8,128)(2,1)} %param.9) | copy-start | bytes 786436
  15.0 30.8 %copy-start.6 = (s32[32]{0:T(128)S(1)}, s32[32]{0:T(128)}, u32[]{:S(2)}) copy-start(s32[32]{0:T(128)} %param.13) | copy-start | bytes 388
  15.0 105.9 %all-to-all-start = ((bf16[32,128,512]{2,1,0:T(8,128)(2,1)}), bf16[32,128,512]{2,1,0:T(8,128)(2,1)}, u32[]{:S(2)}, u32[]{:S(2)}) async-start(bf16[32,128,512]{2,1,0:T(8,128)(2,1)} %broadcast_select_fusion.1), calls=%async_computation | async-start | bytes 8388608 | tf_op jit(solution)/shard_map/all_to_all | solution.py:82
  26.4 5.4 %collective-permute-start = (bf16[1,256,512]{2,1,0:T(8,128)(2,1)S(1)}, bf16[1,256,512]{2,1,0:T(8,128)(2,1)S(1)}, u32[]{:S(2)}, u32[]{:S(2)}) collective-permute-start(bf16[1,256,512]{2,1,0:T(8,128)(2,1)S(1)} %copy-done.2), channel_id=1, source_target_pairs={{0,1},{1,2},{2,3},{3,4},{4,5},{5,6},{6,7},{7,0},{8,9},{9,10},{10,1... | collective-permute-start | bytes 786440 | tf_op jit(solution)/shard_map/ppermute | solution.py:13
  28.4 11.6 %collective-permute-start.4 = (bf16[1,256,512]{2,1,0:T(8,128)(2,1)S(1)}, bf16[1,256,512]{2,1,0:T(8,128)(2,1)S(1)}, u32[]{:S(2)}, u32[]{:S(2)}) collective-permute-start(bf16[1,256,512]{2,1,0:T(8,128)(2,1)S(1)} %copy-done.2), channel_id=1, source_target_pairs={{0,7},{1,0},{2,1},{3,2},{4,3},{5,4},{6,5},{7,6},{8,15},{9,8},{10,9... | collective-permute-start | bytes 786440 | tf_op jit(solution)/shard_map/ppermute | solution.py:15
  31.7 5.8 %collective-permute-start.1 = (bf16[1,256,512]{2,1,0:T(8,128)(2,1)S(1)}, bf16[1,256,512]{2,1,0:T(8,128)(2,1)S(1)}, u32[]{:S(2)}, u32[]{:S(2)}) collective-permute-start(bf16[1,256,512]{2,1,0:T(8,128)(2,1)S(1)} %collective-permute-done), channel_id=1, source_target_pairs={{0,1},{1,2},{2,3},{3,4},{4,5},{5,6},{6,7},{7,0},{8,9},{9,10},{10,1... | collective-permute-start | bytes 786440 | tf_op jit(solution)/shard_map/ppermute | solution.py:13
  37.5 5.8 %collective-permute-start.2 = (bf16[1,256,512]{2,1,0:T(8,128)(2,1)S(1)}, bf16[1,256,512]{2,1,0:T(8,128)(2,1)S(1)}, u32[]{:S(2)}, u32[]{:S(2)}) collective-permute-start(bf16[1,256,512]{2,1,0:T(8,128)(2,1)S(1)} %collective-permute-done.1), channel_id=1, source_target_pairs={{0,1},{1,2},{2,3},{3,4},{4,5},{5,6},{6,7},{7,0},{8,9},{9,10},{10,1... | collective-permute-start | bytes 786440 | tf_op jit(solution)/shard_map/ppermute | solution.py:13
  40.0 9.2 %collective-permute-start.5 = (bf16[1,256,512]{2,1,0:T(8,128)(2,1)S(1)}, bf16[1,256,512]{2,1,0:T(8,128)(2,1)S(1)}, u32[]{:S(2)}, u32[]{:S(2)}) collective-permute-start(bf16[1,256,512]{2,1,0:T(8,128)(2,1)S(1)} %collective-permute-done.4), channel_id=1, source_target_pairs={{0,7},{1,0},{2,1},{3,2},{4,3},{5,4},{6,5},{7,6},{8,15},{9,8},{10,9... | collective-permute-start | bytes 786440 | tf_op jit(solution)/shard_map/ppermute | solution.py:15
  43.3 5.9 %collective-permute-start.3 = (bf16[1,256,512]{2,1,0:T(8,128)(2,1)S(1)}, bf16[1,256,512]{2,1,0:T(8,128)(2,1)S(1)}, u32[]{:S(2)}, u32[]{:S(2)}) collective-permute-start(bf16[1,256,512]{2,1,0:T(8,128)(2,1)S(1)} %collective-permute-done.2), channel_id=1, source_target_pairs={{0,1},{1,2},{2,3},{3,4},{4,5},{5,6},{6,7},{7,0},{8,9},{9,10},{10,1... | collective-permute-start | bytes 786440 | tf_op jit(solution)/shard_map/ppermute | solution.py:13
  49.2 6.2 %collective-permute-start.6 = (bf16[1,256,512]{2,1,0:T(8,128)(2,1)S(1)}, bf16[1,256,512]{2,1,0:T(8,128)(2,1)S(1)}, u32[]{:S(2)}, u32[]{:S(2)}) collective-permute-start(bf16[1,256,512]{2,1,0:T(8,128)(2,1)S(1)} %collective-permute-done.5), channel_id=1, source_target_pairs={{0,7},{1,0},{2,1},{3,2},{4,3},{5,4},{6,5},{7,6},{8,15},{9,8},{10,9... | collective-permute-start | bytes 786440 | tf_op jit(solution)/shard_map/ppermute | solution.py:15
  55.7 1.9 copy-start.1
  60.5 2.8 %copy-start = (bf16[32,128,512]{2,1,0:T(8,128)(2,1)S(1)}, bf16[32,128,512]{2,1,0:T(8,128)(2,1)}, u32[]{:S(2)}) copy-start(bf16[32,128,512]{2,1,0:T(8,128)(2,1)} %gather_fusion.2) | copy-start | bytes 12582916
  120.9 104.3 %all-to-all-start.1 = ((bf16[32,128,512]{2,1,0:T(8,128)(2,1)}), bf16[32,128,512]{2,1,0:T(8,128)(2,1)}, u32[]{:S(2)}, u32[]{:S(2)}) async-start(bf16[32,128,512]{2,1,0:T(8,128)(2,1)} %broadcast_select_fusion), calls=%async_computation.1 | async-start | bytes 8388608 | tf_op jit(solution)/shard_map/all_to_all | solution.py:101
  135.9 89.3 %copy-start.5 = (s32[32]{0:T(128)S(1)}, s32[32]{0:T(128)}, u32[]{:S(2)}) copy-start(s32[32]{0:T(128)} %fusion.41) | copy-start | bytes 388
